TPU v7x, 512 devices: a whole 4x4x16 slice. The times are simulated.
512 devices in a mesh: clip: 4 (over y), st: 32 (over x_hi, z), fsdp: 4 (over x_lo, core).
Axes of the slice: x: 4 (x_hi: 2, x_lo: 2; x = x_hi * 2 + x_lo), y: 4, z: 16, core: 2. Of those that a mesh axis runs over, the one named last changes fastest.
Arguments:
- clip_tokens: bfloat16 [1024, 128, 1024], P(('clip', 'st'), 'fsdp'), parts along dimension 0, may hold values from -6 to 6
- w_spatial: bfloat16 [9, 1024, 512], P(None, ('st', 'fsdp')), may hold values from -0.0625 to 0.0625
- w_temporal: bfloat16 [3, 512, 1024], P(None, None, ('st', 'fsdp')), may hold values from -0.15625 to 0.15625
- frame_time: int32 [64], P('clip'), parts along dimension 0, may hold values from 0 to 15, each once
- dilation: int32 [32], P('clip'), parts along dimension 0, may hold values from 1 to 3
Outputs:
- block_out: bfloat16 [1024, 128, 1024], P(('clip', 'st'), 'fsdp'), parts along dimension 0
There are 4 independent parts, one for each index of `clip`. A program takes and returns all parts, laid end to end along the dimension named above; an argument that names none is the same for every part. Nothing has to cross between parts.
Inputs may be any that keep to these rules, and one draw needn't show every extreme that they name: frame_time is a permutation of 0 to 15.
All inputs are finite; a program needn't handle non-finite values.
Results may differ from a plain program's by a relative error of at most 0.0049.
Values may be sent and summed in bfloat16 or wider, within the bound.
No kernel may reach another device: no remote copies, remote signals or barrier semaphores. Data moves between devices by JAX's collectives and lax.ppermute only.
A program may use at most 64 MiB of HBM per device.

v0:
```python
import jax
import jax.numpy as jnp
from jax import lax
from jax.sharding import PartitionSpec as P

DGROUPS = 8
FRAMES = 16
ROWS = 16


def padded_2(cells, sides, width):
    for axis, dim in sides:
        count = lax.axis_size(axis)
        ends = count - 1
        head = lax.slice_in_dim(cells, 0, width, axis=dim)
        tail = lax.slice_in_dim(cells, cells.shape[dim] - width, cells.shape[dim], axis=dim)
        cells = jnp.concatenate(
            [
                lax.ppermute(tail, axis, [(i, (i + 1) % count) for i in range(ends)]),
                cells,
                lax.ppermute(head, axis, [((i + 1) % count, i) for i in range(ends)]),
            ],
            axis=dim,
        )
    return cells


def partner(value, axis, distance):
    mask = 2**distance
    pairs = [(source, source ^ mask) for source in range(lax.axis_size(axis))]
    return lax.ppermute(value, axis, pairs)


def shards(clip_tokens, w_spatial, w_temporal, frame_time, dilation):
    rows_dev, cols_dev, channels = clip_tokens.shape
    middle = w_spatial.shape[2]
    group_size = lax.axis_size("st")
    values = clip_tokens.astype(jnp.float32)
    average = jnp.mean(values, axis=-1, keepdims=True)
    kernel_extent = jnp.mean(jnp.square(values - average), axis=-1, keepdims=True)
    normed = ((values - average) * lax.rsqrt(kernel_extent + 1e-06)).astype(jnp.bfloat16)
    widened = padded_2(normed, (("fsdp", 1),), 1)
    blank_row = jnp.zeros((1,) + widened.shape[1:], jnp.bfloat16)
    lower_half = lax.axis_index("st") % 2 == 1
    outgoing = jnp.where(lower_half, widened[:1], widened[-1:])
    incoming = partner(outgoing, "st", 0)
    top_rim = jnp.where(lower_half, incoming, blank_row)
    bottom_rim = jnp.where(lower_half, blank_row, incoming)
    padded = jnp.concatenate([top_rim, widened, bottom_rim], axis=0)
    first_row = lax.axis_index("st") * rows_dev
    in_frame = (first_row + jnp.arange(rows_dev, dtype=jnp.int32)) % ROWS
    windows = []
    for shift_amount in (-1, 0, 1):
        inside = ((in_frame + shift_amount >= 0) & (in_frame + shift_amount < ROWS)).astype(
            jnp.bfloat16
        )
        windows.append(
            padded[1 + shift_amount : 1 + shift_amount + rows_dev] * inside[:, None, None]
        )
    tokens = rows_dev * cols_dev
    initial = jnp.zeros((tokens, middle), jnp.float32)
    running = initial
    portion = lax.all_gather(w_spatial, ("st", "fsdp"), axis=1, tiled=True)
    span = portion.shape[1]
    for row_tap in range(3):
        for column_kernel_tap in range(3):
            patches = windows[row_tap][:, column_kernel_tap : column_kernel_tap + cols_dev, :]
            running = running + jnp.dot(
                patches.reshape(tokens, span),
                portion[3 * row_tap + column_kernel_tap],
                preferred_element_type=jnp.float32,
            )
    hidden = jax.nn.gelu(running).astype(jnp.bfloat16)
    pixel_values = ROWS * cols_dev
    block_length_span = min(tokens, pixel_values) // group_size
    depth_len = tokens // (group_size * block_length_span)
    arrived = lax.all_to_all(
        hidden.reshape(depth_len, group_size, block_length_span, middle),
        "st",
        split_axis=1,
        concat_axis=0,
        tiled=True,
    )
    per_pixel = pixel_values // group_size
    group_width = middle // DGROUPS
    frame_sequence = arrived.reshape(FRAMES, per_pixel, DGROUPS, group_width)
    offsets = (jnp.arange(3, dtype=jnp.int32) - 1)[None, :] * dilation[:, None]
    selector_matrix = (
        frame_time[None, None, None, :]
        == frame_time[None, None, :, None] + offsets[:, :, None, None]
    ).astype(jnp.bfloat16)
    stacked_panels = jnp.einsum(
        "gkfe,epgc->kfpgc", selector_matrix, frame_sequence, preferred_element_type=jnp.float32
    )
    stacked_panels = stacked_panels.astype(jnp.bfloat16).reshape(3, FRAMES * per_pixel, middle)
    portion = lax.all_gather(w_temporal, ("st", "fsdp"), axis=2, tiled=True)
    result = jnp.dot(stacked_panels[0], portion[0], preferred_element_type=jnp.float32)
    result = result + jnp.dot(stacked_panels[1], portion[1], preferred_element_type=jnp.float32)
    mixed_out = (
        result + jnp.dot(stacked_panels[2], portion[2], preferred_element_type=jnp.float32)
    ).astype(jnp.bfloat16)
    returned = lax.all_to_all(
        mixed_out.reshape(group_size, depth_len, 1, block_length_span, channels),
        "st",
        split_axis=0,
        concat_axis=2,
        tiled=True,
    )
    update = returned.reshape(rows_dev, cols_dev, channels)
    return (values + update.astype(jnp.float32)).astype(jnp.bfloat16)


def solution(mesh):
    return jax.shard_map(
        shards,
        mesh=mesh,
        in_specs=(
            P(("clip", "st"), "fsdp", None),
            P(None, ("st", "fsdp"), None),
            P(None, None, ("st", "fsdp")),
            P("clip"),
            P("clip"),
        ),
        out_specs=P(("clip", "st"), "fsdp", None),
        check_vma=False,
    )
```

profile of v0, /device:TPU:32, one launch (start us, length us, event | category | flops | bytes accessed | tf_op | source)
XLA Modules:
  0.0 523.0 jit_solution(9462733615842802531)
XLA Ops:
  6.5 0.7 all-gather.3.cloned.1.call-update
  7.3 0.0 all-gather.5.cloned.1.call-start
  7.3 0.7 all-gather.5.cloned.1.call-update
  8.0 1.2 convert_reduce_fusion
  9.2 1.3 fusion.5
  10.5 1.3 fusion.6
  11.8 0.1 fusion.31
  11.9 1.7 collective-permute-start
  13.7 1.3 collective-permute-start.1
  15.0 3.0 collective-permute-done.1
  18.0 0.2 pad_maximum_fusion.6
  18.3 5.7 %collective-permute-start.2 = (bf16[1,34,1024]{2,1,0:T(8,128)(2,1)S(1)}, bf16[1,34,1024]{2,1,0:T(8,128)(2,1)S(1)}, u32[]{:S(2)}, u32[]{:S(2)}) collective-permute-start(bf16[1,34,1024]{2,1,0:T(8,128)(2,1)S(1)} %slice_select_fusion), channel_id=1, source_target_pairs={{0,4},{4,0},{8,12},{12,8},{16,20},{20,16},{24,28},{28,24},{32,36},... | collective-permute-start | bytes 208904 | tf_op jit(solution)/shard_map/ppermute | solution.py:31
  24.0 3.2 collective-permute-done.2
  27.2 0.7 fusion.10
  27.9 1.2 fusion.30
  29.1 0.3 fusion.29
  29.4 1.1 fusion.28
  30.5 212.5 %all-gather.3.cloned.1.call-done = bf16[9,1024,512]{2,1,0:T(8,128)(2,1)} async-done(((bf16[9,8,512]{2,1,0:T(8,128)(2,1)}), bf16[9,1024,512]{2,1,0:T(8,128)(2,1)}) %all-gather.3.cloned.1.call-update) | async-done | bytes 9437200 | tf_op jit(solution)/shard_map/all_gather | solution.py:63
  243.0 2.0 fusion.9
  244.9 2.4 convolution_add_fusion.9
  247.3 1.7 convolution_add_fusion.8
  249.0 1.7 convolution_add_fusion.7
  250.7 0.4 convolution_add_fusion.6
  251.1 0.4 convolution_add_fusion.5
  251.6 0.4 convolution_add_fusion.4
  252.0 0.4 convolution_add_fusion.3
  252.5 0.6 copy-done.3
  253.1 1.3 fusion.20
  254.3 11.1 %all-to-all-start = ((bf16[1,32,8,512]{3,2,0,1:T(8,128)(2,1)}), bf16[1,32,8,512]{3,2,0,1:T(8,128)(2,1)S(1)}, u32[]{:S(2)}, u32[]{:S(2)}) async-start(bf16[1,32,8,512]{3,2,0,1:T(8,128)(2,1)} %fusion.20), calls=%async_computation | async-start | bytes 524288 | tf_op jit(solution)/shard_map/all_to_all | solution.py:77
  265.5 0.1 broadcast_multiply_fusion.1
  265.6 0.1 broadcast_add_fusion
  265.7 21.6 %all-to-all-done = bf16[1,32,8,512]{3,2,0,1:T(8,128)(2,1)S(1)} async-done(((bf16[1,32,8,512]{3,2,0,1:T(8,128)(2,1)}), bf16[1,32,8,512]{3,2,0,1:T(8,128)(2,1)S(1)}, u32[]{:S(2)}, u32[]{:S(2)}) %all-to-all-start) | async-done | bytes 262176 | tf_op jit(solution)/shard_map/all_to_all | solution.py:77
  287.3 0.3 reshape.149
  287.6 0.9 fusion
  288.4 0.3 fusion.27
  288.7 0.3 copy.12
  289.1 0.3 squeeze.54
  289.4 0.3 copy.13
  289.7 0.3 squeeze.56
  290.1 0.3 copy.14
  290.4 0.3 squeeze.58
  290.7 176.7 %all-gather.5.cloned.1.call-done = bf16[3,512,1024]{1,2,0:T(8,128)(2,1)} async-done(((bf16[3,512,8]{1,2,0:T(8,128)(2,1)}), bf16[3,512,1024]{1,2,0:T(8,128)(2,1)}) %all-gather.5.cloned.1.call-update) | async-done | bytes 3145744 | tf_op jit(solution)/shard_map/all_gather | solution.py:96
  467.4 1.7 fusion.8
  469.1 1.7 convolution_add_fusion.1
  470.8 0.0 copy-start
  470.8 1.7 fusion.4
  472.6 42.6 %all_to_all.8 = bf16[32,1,1,8,1024]{4,3,2,1,0:T(8,128)(2,1)S(1)} all-to-all(bf16[32,1,1,8,1024]{4,3,2,1,0:T(8,128)(2,1)S(1)} %fusion.4), channel_id=1, replica_groups=mesh['clip'=4,'st'=32,'fsdp'=4] {'st'}, dimensions={0} | all-to-all | bytes 1048576 | tf_op jit(solution)/shard_map/all_to_all | solution.py:102
  515.2 1.0 fusion.7
  (19 shorter events, 0.1 us)
Async XLA Ops:
  6.5 236.4 %all-gather.3.cloned.1.call-start = ((), (), s32[]{:S(2)}) async-start(), calls=%async_computation.2 | async-start | bytes 9510912 | tf_op jit(solution)/shard_map/all_gather | solution.py:63
  7.3 460.2 %all-gather.5.cloned.1.call-start = ((), (), s32[]{:S(2)}) async-start(), calls=%async_computation.3 | async-start | bytes 3170304 | tf_op jit(solution)/shard_map/all_gather | solution.py:96
  11.9 3.1 collective-permute-start
  13.7 4.4 collective-permute-start.1
  18.3 8.9 %collective-permute-start.2 = (bf16[1,34,1024]{2,1,0:T(8,128)(2,1)S(1)}, bf16[1,34,1024]{2,1,0:T(8,128)(2,1)S(1)}, u32[]{:S(2)}, u32[]{:S(2)}) collective-permute-start(bf16[1,34,1024]{2,1,0:T(8,128)(2,1)S(1)} %slice_select_fusion), channel_id=1, source_target_pairs={{0,4},{4,0},{8,12},{12,8},{16,20},{20,16},{24,28},{28,24},{32,36},... | collective-permute-start | bytes 208904 | tf_op jit(solution)/shard_map/ppermute | solution.py:31
  242.9 2.0 copy-start.2
  242.9 7.7 %copy-start.1 = (bf16[9,1024,512]{2,1,0:T(8,128)(2,1)S(1)}, bf16[9,1024,512]{2,1,0:T(8,128)(2,1)}, u32[]{:S(2)}) copy-start(bf16[9,1024,512]{2,1,0:T(8,128)(2,1)} %all-gather.3.cloned.1.call-done) | copy-start | bytes 28311556
  252.0 1.0 copy-start.3
  253.1 12.4 %copy-start.5 = (s32[8]{0:T(128)S(1)}, s32[8]{0:T(128)}, u32[]{:S(2)}) copy-start(s32[8]{0:T(128)} %param.9) | copy-start | bytes 100
  253.1 12.5 %copy-start.4 = (s32[16]{0:T(128)S(1)}, s32[16]{0:T(128)}, u32[]{:S(2)}) copy-start(s32[16]{0:T(128)} %param.8) | copy-start | bytes 196
  254.3 33.0 %all-to-all-start = ((bf16[1,32,8,512]{3,2,0,1:T(8,128)(2,1)}), bf16[1,32,8,512]{3,2,0,1:T(8,128)(2,1)S(1)}, u32[]{:S(2)}, u32[]{:S(2)}) async-start(bf16[1,32,8,512]{3,2,0,1:T(8,128)(2,1)} %fusion.20), calls=%async_computation | async-start | bytes 524288 | tf_op jit(solution)/shard_map/all_to_all | solution.py:77
  470.8 44.4 %copy-start = (bf16[8,32,1024]{2,1,0:T(8,128)(2,1)S(1)}, bf16[8,32,1024]{2,1,0:T(8,128)(2,1)}, u32[]{:S(2)}) copy-start(bf16[8,32,1024]{2,1,0:T(8,128)(2,1)} %param.5) | copy-start | bytes 1572868
Sparse Core Ops, SparseCore 0:
  9.5 233.3 all-gather.2
  245.1 222.2 all-gather.4
where the time goes:
time: 524 us; the launch traced here: 523 us
  waiting for transfers between devices  418 us (80%)
  blocking collectives  42.6 us (8%)
  starting transfers between devices  19.9 us (4%)
  matrix products  16.7 us (3%)
  between operations  13.7 us (3%)
  other arithmetic  5.9 us (1%)
  local copies, waits for them, and re-layouts  5.82 us (1%)
    all_gather x1, waiting for transfers between devices, shards(): portion = lax.all_gather(w_spatial, ('st', 'fsdp'), axis=1, tiled=True)  212 us
    all_gather x1, waiting for transfers between devices, shards(): portion = lax.all_gather(w_temporal, ('st', 'fsdp'), axis=2, tiled=True)  177 us
    all_to_all x1, blocking collectives, shards(): lax.all_to_all(mixed_out.reshape(group_size, depth_len, 1, block_length_s...  42.6 us
    all_to_all x1, waiting for transfers between devices, shards(): lax.all_to_all(hidden.reshape(depth_len, group_size, block_length_span, m...  21.6 us
    all_to_all x1, starting transfers between devices, shards(): lax.all_to_all(hidden.reshape(depth_len, group_size, block_length_span, m...  11.1 us
    dot_general x9, matrix products, shards(): jnp.dot(patches.reshape(tokens, span), portion[3 * row_tap + column_kerne...  10.7 us
  transfers between devices with their start and end apart: 6, of which 5 were waited for; matrix products, arithmetic and copies ran while one was open for 4% of the time, Pallas kernels for 0%

commit v1 on v0

--- a/solution.py
+++ b/solution.py
@@ -60,7 +60,12 @@
     tokens = rows_dev * cols_dev
     initial = jnp.zeros((tokens, middle), jnp.float32)
     running = initial
-    portion = lax.all_gather(w_spatial, ("st", "fsdp"), axis=1, tiled=True)
+    portion = jnp.concatenate(
+        lax.all_to_all(
+            jnp.stack([w_spatial] * lax.axis_size(("st", "fsdp"))), ("st", "fsdp"), 0, 0
+        ),
+        axis=1,
+    )
     span = portion.shape[1]
     for row_tap in range(3):
         for column_kernel_tap in range(3):

time: 524 us -> 566 us (1.080)
  the two profiles are of different devices: /device:TPU:32 before, /device:TPU:58 now
where the time goes in v1:
time: 566 us; the launch traced here: 565 us
  waiting for transfers between devices  432 us (76%)
  starting transfers between devices  46.5 us (8%)
  blocking collectives  37.6 us (7%)
  matrix products  22 us (4%)
  between operations  13.8 us (2%)
  local copies, waits for them, and re-layouts  10.4 us (2%)
    ppermute x1, waiting for transfers between devices, partner(): return lax.ppermute(value, axis, pairs)  380 us
    all_to_all x1, blocking collectives, shards(): lax.all_to_all(mixed_out.reshape(group_size, depth_len, 1, block_length_s...  37.6 us
    all_to_all x1, waiting for transfers between devices, shards(): lax.all_to_all(jnp.stack([w_spatial] * lax.axis_size(('st', 'fsdp'))), ('...  23.7 us
    all_to_all x1, waiting for transfers between devices, shards(): lax.all_to_all(hidden.reshape(depth_len, group_size, block_length_span, m...  22.5 us
    all_to_all x1, starting transfers between devices, shards(): lax.all_to_all(jnp.stack([w_spatial] * lax.axis_size(('st', 'fsdp'))), ('...  19.5 us
    all_to_all x1, starting transfers between devices, shards(): lax.all_to_all(hidden.reshape(depth_len, group_size, block_length_span, m...  19.5 us
    dot_general x9, matrix products, shards(): jnp.dot(patches.reshape(tokens, span), portion[3 * row_tap + column_kerne...  16.1 us
  transfers between devices with their start and end apart: 6, of which 4 were waited for; matrix products, arithmetic and copies ran while one was open for 4% of the time, Pallas kernels for 0%

profile of v1, /device:TPU:58, one launch (start us, length us, event | category | flops | bytes accessed | tf_op | source)
XLA Modules:
  0.0 565.0 jit_solution(4320037018576249620)
XLA Ops:
  6.5 5.1 stack.2
  11.7 19.5 %all-to-all-start = ((bf16[128,9,8,512]{3,2,1,0:T(8,128)(2,1)}), bf16[128,9,8,512]{3,2,1,0:T(8,128)(2,1)}, u32[]{:S(2)}, u32[]{:S(2)}) async-start(bf16[128,9,8,512]{3,2,1,0:T(8,128)(2,1)} %stack.2), calls=%async_computation | async-start | bytes 18874368 | tf_op jit(solution)/shard_map/all_to_all | solution.py:64
  31.2 0.0 all-gather.2.cloned.1.call-start
  31.2 0.7 all-gather.2.cloned.1.call-update
  31.9 0.1 convert_reduce_fusion
  32.1 0.3 fusion.5
  32.4 0.3 fusion.6
  32.7 0.1 fusion.31
  32.7 2.1 collective-permute-start
  34.8 3.5 collective-permute-start.1
  38.3 4.7 collective-permute-done
  43.1 0.2 pad_maximum_fusion.6
  43.3 1.9 collective-permute-start.2
  45.3 380.4 %collective-permute-done.2 = bf16[1,34,1024]{2,1,0:T(8,128)(2,1)S(1)} collective-permute-done((bf16[1,34,1024]{2,1,0:T(8,128)(2,1)S(1)}, bf16[1,34,1024]{2,1,0:T(8,128)(2,1)S(1)}, u32[]{:S(2)}, u32[]{:S(2)}) %collective-permute-start.2) | collective-permute-done | bytes 69664 | tf_op jit(solution)/shard_map/ppermute | solution.py:31
  425.7 0.7 fusion.10
  426.4 1.3 fusion.30
  427.7 0.3 fusion.29
  427.9 1.1 fusion.28
  429.0 23.7 %all-to-all-done = bf16[128,9,8,512]{3,2,1,0:T(8,128)(2,1)} async-done(((bf16[128,9,8,512]{3,2,1,0:T(8,128)(2,1)}), bf16[128,9,8,512]{3,2,1,0:T(8,128)(2,1)}, u32[]{:S(2)}, u32[]{:S(2)}) %all-to-all-start) | async-done | bytes 9437216 | tf_op jit(solution)/shard_map/all_to_all | solution.py:64
  452.7 1.9 fusion.9
  454.6 0.0 copy-start.1
  454.6 1.7 convolution_add_fusion.9
  456.3 1.7 convolution_add_fusion.8
  458.0 1.7 convolution_add_fusion.7
  459.6 1.7 convolution_add_fusion.6
  461.3 1.7 convolution_add_fusion.5
  463.0 1.7 convolution_add_fusion.4
  464.6 1.7 convolution_add_fusion.3
  466.4 2.5 fusion.20
  468.9 19.5 %all-to-all-start.1 = ((bf16[1,32,8,512]{3,2,0,1:T(8,128)(2,1)}), bf16[1,32,8,512]{3,2,0,1:T(8,128)(2,1)S(1)}, u32[]{:S(2)}, u32[]{:S(2)}) async-start(bf16[1,32,8,512]{3,2,0,1:T(8,128)(2,1)} %fusion.20), calls=%async_computation.1 | async-start | bytes 524288 | tf_op jit(solution)/shard_map/all_to_all | solution.py:82
  488.4 0.1 broadcast_multiply_fusion.1
  488.5 0.1 broadcast_add_fusion
  488.5 22.5 %all-to-all-done.1 = bf16[1,32,8,512]{3,2,0,1:T(8,128)(2,1)S(1)} async-done(((bf16[1,32,8,512]{3,2,0,1:T(8,128)(2,1)}), bf16[1,32,8,512]{3,2,0,1:T(8,128)(2,1)S(1)}, u32[]{:S(2)}, u32[]{:S(2)}) %all-to-all-start.1) | async-done | bytes 262176 | tf_op jit(solution)/shard_map/all_to_all | solution.py:82
  511.0 0.3 reshape.174
  511.3 0.9 fusion
  512.1 0.3 fusion.27
  512.4 0.3 copy.12
  512.8 0.3 squeeze.54
  513.1 0.3 copy.13
  513.4 0.3 squeeze.56
  513.8 0.3 copy.14
  514.1 0.3 squeeze.58
  514.4 0.0 all-gather.2.cloned.1.call-done
  514.5 1.7 fusion.8
  516.2 1.7 convolution_add_fusion.1
  517.9 1.7 fusion.4
  519.6 37.6 %all_to_all.23 = bf16[32,1,1,8,1024]{4,3,2,1,0:T(8,128)(2,1)S(1)} all-to-all(bf16[32,1,1,8,1024]{4,3,2,1,0:T(8,128)(2,1)S(1)} %fusion.4), channel_id=1, replica_groups=mesh['clip'=4,'st'=32,'fsdp'=4] {'st'}, dimensions={0} | all-to-all | bytes 1048576 | tf_op jit(solution)/shard_map/all_to_all | solution.py:107
  557.2 1.0 fusion.7
  (19 shorter events, 0.1 us)
Async XLA Ops:
  11.7 20.3 %copy-start = (bf16[8,32,1024]{2,1,0:T(8,128)(2,1)S(1)}, bf16[8,32,1024]{2,1,0:T(8,128)(2,1)}, u32[]{:S(2)}) copy-start(bf16[8,32,1024]{2,1,0:T(8,128)(2,1)} %param.5) | copy-start | bytes 1572868
  11.7 441.0 %all-to-all-start = ((bf16[128,9,8,512]{3,2,1,0:T(8,128)(2,1)}), bf16[128,9,8,512]{3,2,1,0:T(8,128)(2,1)}, u32[]{:S(2)}, u32[]{:S(2)}) async-start(bf16[128,9,8,512]{3,2,1,0:T(8,128)(2,1)} %stack.2), calls=%async_computation | async-start | bytes 18874368 | tf_op jit(solution)/shard_map/all_to_all | solution.py:64
  31.2 483.3 %all-gather.2.cloned.1.call-start = ((), (), s32[]{:S(2)}) async-start(), calls=%async_computation.3 | async-start | bytes 3170304 | tf_op jit(solution)/shard_map/all_gather | solution.py:101
  32.7 10.3 %collective-permute-start = (bf16[8,1,1024]{2,1,0:T(2,128)(2,1)S(1)}, bf16[8,1,1024]{2,1,0:T(2,128)(2,1)S(1)}, u32[]{:S(2)}, u32[]{:S(2)}) collective-permute-start(bf16[8,1,1024]{2,1,0:T(2,128)(2,1)S(1)} %get-tuple-element.20), channel_id=1, source_target_pairs={{0,1},{1,2},{2,3},{4,5},{5,6},{6,7},{8,9},{9,10},{10,11},{12,13},{... | collective-permute-start | bytes 49160 | tf_op jit(solution)/shard_map/ppermute | solution.py:19
  34.8 8.3 %collective-permute-start.1 = (bf16[8,1,1024]{2,1,0:T(2,128)(2,1)S(1)}, bf16[8,1,1024]{2,1,0:T(2,128)(2,1)S(1)}, u32[]{:S(2)}, u32[]{:S(2)}) collective-permute-start(bf16[8,1,1024]{2,1,0:T(2,128)(2,1)S(1)} %get-tuple-element.21), channel_id=1, source_target_pairs={{1,0},{2,1},{3,2},{5,4},{6,5},{7,6},{9,8},{10,9},{11,10},{13,12},{... | collective-permute-start | bytes 49160 | tf_op jit(solution)/shard_map/ppermute | solution.py:21
  43.3 382.3 %collective-permute-start.2 = (bf16[1,34,1024]{2,1,0:T(8,128)(2,1)S(1)}, bf16[1,34,1024]{2,1,0:T(8,128)(2,1)S(1)}, u32[]{:S(2)}, u32[]{:S(2)}) collective-permute-start(bf16[1,34,1024]{2,1,0:T(8,128)(2,1)S(1)} %slice_select_fusion), channel_id=1, source_target_pairs={{0,4},{4,0},{8,12},{12,8},{16,20},{20,16},{24,28},{28,24},{32,36},... | collective-permute-start | bytes 208904 | tf_op jit(solution)/shard_map/ppermute | solution.py:31
  452.7 1.9 copy-start.2
  454.6 1.7 copy-start.1
  464.6 1.7 copy-start.3
  466.4 22.0 %copy-start.5 = (s32[8]{0:T(128)S(1)}, s32[8]{0:T(128)}, u32[]{:S(2)}) copy-start(s32[8]{0:T(128)} %param.9) | copy-start | bytes 100
  466.4 22.1 %copy-start.4 = (s32[16]{0:T(128)S(1)}, s32[16]{0:T(128)}, u32[]{:S(2)}) copy-start(s32[16]{0:T(128)} %param.8) | copy-start | bytes 196
  468.9 42.1 %all-to-all-start.1 = ((bf16[1,32,8,512]{3,2,0,1:T(8,128)(2,1)}), bf16[1,32,8,512]{3,2,0,1:T(8,128)(2,1)S(1)}, u32[]{:S(2)}, u32[]{:S(2)}) async-start(bf16[1,32,8,512]{3,2,0,1:T(8,128)(2,1)} %fusion.20), calls=%async_computation.1 | async-start | bytes 524288 | tf_op jit(solution)/shard_map/all_to_all | solution.py:82
Sparse Core Ops, SparseCore 0:
  34.2 342.1 all-gather.1
